TPU v7x, 256 devices: a whole 4x4x8 slice. The times are simulated.
256 devices in a mesh: dp: 8 (over x, core), ctx: 32 (over z, y).
Axes of the slice: x: 4, y: 4, z: 8, core: 2. Of those that a mesh axis runs over, the one named last changes fastest.
Arguments:
- features: bfloat16 [8, 8192, 2560], P('dp', 'ctx'), may hold values from -5 to 5
- step_logits: float32 [8, 40, 8192], P('dp', None, 'ctx'), may hold values from -4 to 4
- writer: bfloat16 [8, 8192, 128], P('dp', 'ctx'), may hold values from -5 to 5
- reader: bfloat16 [8, 8192, 128], P('dp', 'ctx'), may hold values from -5 to 5
- log_rates: float32 [40], replicated, may hold values from -3 to 1
- step_bias: float32 [40], replicated, may hold values from -7 to -2
- skip_gain: float32 [40], replicated, may hold values from 0.5 to 1.5
- document_lengths: int32 [8, 4], P('dp'), may hold values from 1 to 4096, 8192 in all within a row
- cotangent: bfloat16 [8, 8192, 2560], P('dp', 'ctx'), may hold values from -5 to 5
Outputs:
- features_gradient: bfloat16 [8, 8192, 2560], P('dp', 'ctx')
- steps_gradient: float32 [8, 40, 8192], P('dp', None, 'ctx')
- writer_gradient: float32 [8, 8192, 128], P('dp', 'ctx')
- reader_gradient: float32 [8, 8192, 128], P('dp', 'ctx')
- head_gradient: float32 [3, 40], replicated
Inputs may be any that keep to these rules, and one draw needn't show every extreme that they name: `document_lengths`: each row holds the lengths of 4 documents that sum to 8192; the longest of each row is exactly 4096.
All inputs are finite; a program needn't handle non-finite values.
Results may differ from a plain program's by a relative error of at most 0.001.
Values sent between devices are 32-bit elements; how exact they have to be, the bound alone decides.
No kernel may reach another device: no remote copies, remote signals or barrier semaphores. Data moves between devices by JAX's collectives and lax.ppermute only.
A program may use at most 256 MiB of HBM per device.

v0:
```python
import jax
import jax.numpy as jnp
from jax import lax
from jax.experimental import pallas as pl
from jax.sharding import PartitionSpec as P

SPAN = 256


HIGH = lax.Precision.HIGHEST


def forward_kernel(moved_ref, decay_ref, out_ref):
    def step(j, state):
        out_ref[j] = state
        return decay_ref[j] * state + moved_ref[j]

    lax.fori_loop(0, moved_ref.shape[0], step, jnp.zeros(out_ref.shape[1:], jnp.float32))


def backward_kernel(moved_ref, decay_ref, out_ref):
    count = moved_ref.shape[0]

    def step(k, pull):
        j = count - 1 - k
        out_ref[j] = pull
        return decay_ref[j] * pull + moved_ref[j]

    lax.fori_loop(0, count, step, jnp.zeros(out_ref.shape[1:], jnp.float32))


def exchange_scan(through, local_state, local_pull, axis):
    count = lax.axis_size(axis)
    rows, width = local_state.shape
    heads = through.shape[0]
    half = count // 2
    part = rows // half
    sent = jnp.concatenate(
        [
            local_state.reshape(half, part, width),
            local_pull.reshape(half, part, width),
        ],
        axis=0,
    )
    spare = 128 * ((heads + 127) // 128)
    extra = jnp.zeros((count, part, spare), jnp.float32).at[:, 0, :heads].set(through[None, :])
    moved = lax.all_to_all(jnp.concatenate([sent, extra], axis=2), axis, 0, 0, tiled=True)
    decays = jnp.repeat(moved[:, 0, width : width + heads], width // heads, axis=1)[:, None, :]
    lanes = 512 if width % 512 == 0 else width

    def scan_with(kernel):
        return pl.pallas_call(
            kernel,
            out_shape=jax.ShapeDtypeStruct((count, part, width), jnp.float32),
            grid=(width // lanes,),
            in_specs=[
                pl.BlockSpec((count, part, lanes), lambda c: (0, 0, c)),
                pl.BlockSpec((count, 1, lanes), lambda c: (0, 0, c)),
            ],
            out_specs=pl.BlockSpec((count, part, lanes), lambda c: (0, 0, c)),
        )

    scanned = lax.cond(
        lax.axis_index(axis) < half,
        scan_with(forward_kernel),
        scan_with(backward_kernel),
        moved,
        decays,
    )
    back = lax.all_to_all(scanned, axis, 0, 0, tiled=True)
    return back[:half].reshape(rows, width), back[half:].reshape(rows, width)


def group_step(
    state,
    prior_segment,
    inputs,
    log_decay,
    step_size,
    scores,
    reader_piece,
    writer_piece,
    segment_piece,
    skip_gain,
):
    size = inputs.shape[0]
    cumulative = jnp.cumsum(log_decay, axis=1)
    causal = jnp.arange(size)[:, None] >= jnp.arange(size)[None, :]
    within = causal & (segment_piece[:, None] == segment_piece[None, :])
    spread = cumulative[:, :, None] - cumulative[:, None, :]
    decay = jnp.where(within[None], jnp.exp(jnp.where(within[None], spread, 0.0)), 0.0)
    weights = decay * scores[None] * step_size[:, None, :]
    inner = jnp.einsum("hts,shp->thp", weights, inputs, precision=HIGH)
    carry_in = jnp.where((segment_piece == prior_segment)[None], jnp.exp(cumulative), 0.0)
    rows, heads, head_size = state.shape
    from_state = (
        jnp.dot(reader_piece, state.reshape(rows, heads * head_size), precision=HIGH).reshape(
            size, heads, head_size
        )
        * carry_in.T[:, :, None]
    )
    result = inner + from_state + skip_gain[None, :, None] * inputs
    to_end = (
        jnp.where(
            (segment_piece == segment_piece[-1])[None],
            jnp.exp(cumulative[:, -1:] - cumulative),
            0.0,
        )
        * step_size
    )
    fresh = jnp.dot(
        writer_piece.T, (to_end.T[:, :, None] * inputs).reshape(size, heads * head_size), precision=HIGH
    ).reshape(rows, heads, head_size)
    new_state = carry_in[:, -1][None, :, None] * state + fresh
    return (result, new_state)


def shards(
    features,
    step_logits,
    writer,
    reader,
    log_rates,
    step_bias,
    skip_gain,
    document_lengths,
    cotangent,
):
    tokens = features.shape[1]
    width = features.shape[2]
    heads = log_rates.shape[0]
    head_size = width // heads
    state_rows = writer.shape[2]
    span = min(SPAN, tokens)
    blocks = tokens // span
    position = lax.axis_index("ctx") * tokens + jnp.arange(tokens, dtype=jnp.int32)
    starts = jnp.cumsum(document_lengths[0])[:-1]
    segment = jnp.sum(position[:, None] >= starts[None, :], axis=1)
    prior_segment = jnp.sum(position[0] - 1 >= starts)
    inputs = features[0].astype(jnp.float32).reshape(tokens, heads, head_size)
    writer_full = writer[0].astype(jnp.float32)
    reader_full = reader[0].astype(jnp.float32)
    upstream = cotangent[0].astype(jnp.float32).reshape(tokens, heads, head_size)
    all_scores = jnp.einsum(
        "ctn,csn->cts",
        reader[0].reshape(blocks, span, state_rows),
        writer[0].reshape(blocks, span, state_rows),
        preferred_element_type=jnp.float32,
    )
    step_size = jax.nn.softplus(step_logits[0] + step_bias[:, None])
    log_decay = -jnp.exp(log_rates)[:, None] * step_size
    cumulative = jnp.cumsum(log_decay, axis=1)
    from_start = jnp.where((segment == prior_segment)[None], jnp.exp(cumulative), 0.0)
    through = from_start[:, -1]
    to_end = (
        jnp.where((segment == segment[-1])[None], jnp.exp(cumulative[:, -1:] - cumulative), 0.0)
        * step_size
    )
    local_state = jnp.dot(
        writer_full.T, (to_end.T[:, :, None] * inputs).reshape(tokens, width), precision=HIGH
    )
    local_pull = jnp.dot(
        reader_full.T, (from_start.T[:, :, None] * upstream).reshape(tokens, width), precision=HIGH
    )
    start_state, end_pull = exchange_scan(through, local_state, local_pull, "ctx")
    stepper = group_step

    def forward(inputs_in, logits, writer_in, reader_in, scores_in, rates, bias, gain):
        sizes_in = jax.nn.softplus(logits + bias[:, None])
        decays_in = -jnp.exp(rates)[:, None] * sizes_in
        state = start_state.reshape(state_rows, heads, head_size)
        prior = prior_segment
        results = []
        for number in range(blocks):
            first = number * span
            final = first + span
            result, state = stepper(
                state,
                prior,
                inputs_in[first:final],
                decays_in[:, first:final],
                sizes_in[:, first:final],
                scores_in[number],
                reader_in[first:final],
                writer_in[first:final],
                segment[first:final],
                gain,
            )
            prior = segment[final - 1]
            results.append(result)
        return (jnp.concatenate(results, axis=0), state)

    _, pullback = jax.vjp(
        forward,
        inputs,
        step_logits[0],
        writer_full,
        reader_full,
        all_scores,
        log_rates,
        step_bias,
        skip_gain,
    )
    grads = pullback((upstream, end_pull.reshape(state_rows, heads, head_size)))
    score_grads = grads[4]
    reader_extra = jnp.einsum(
        "cts,csn->ctn", score_grads, writer_full.reshape(blocks, span, state_rows), precision=HIGH
    ).reshape(tokens, state_rows)
    writer_extra = jnp.einsum(
        "cts,ctn->csn", score_grads, reader_full.reshape(blocks, span, state_rows), precision=HIGH
    ).reshape(tokens, state_rows)
    factor = float(lax.axis_size("dp") * lax.axis_size("ctx") * tokens) ** (-0.5)
    head_terms = jnp.stack([grads[5], grads[6], grads[7]]) * factor
    devices = lax.axis_size("dp") * lax.axis_size("ctx")
    flat = head_terms.reshape(-1)
    lanes = 128 * ((flat.shape[0] + 127) // 128)
    spread = jnp.broadcast_to(jnp.pad(flat, (0, lanes - flat.shape[0]))[None], (devices, lanes))
    summed = jnp.sum(lax.all_to_all(spread, ("dp", "ctx"), 0, 0, tiled=True), axis=0)
    head_total = summed[: flat.shape[0]].reshape(head_terms.shape)
    features_gradient = grads[0].reshape(tokens, width).astype(jnp.bfloat16)[None]
    return (
        features_gradient,
        grads[1][None],
        (grads[2] + writer_extra)[None],
        (grads[3] + reader_extra)[None],
        head_total,
    )


def solution(mesh):
    placed = (
        P("dp", "ctx", None),
        P("dp", None, "ctx"),
        P("dp", "ctx", None),
        P("dp", "ctx", None),
        P(),
        P(),
        P(),
        P("dp", None),
        P("dp", "ctx", None),
    )
    return jax.shard_map(
        shards,
        mesh=mesh,
        in_specs=placed,
        out_specs=(
            P("dp", "ctx", None),
            P("dp", None, "ctx"),
            P("dp", "ctx", None),
            P("dp", "ctx", None),
            P(),
        ),
        check_vma=False,
    )
```

profile of v0, /device:TPU:1, one launch (start us, length us, event | category | flops | bytes accessed | tf_op | source)
XLA Modules:
  0.0 229.8 jit_solution(9360998176963200487)
XLA Ops:
  0.6 0.7 exponential_negate_fusion
  1.3 0.8 squeeze.28
  2.2 0.8 fusion.56
  2.9 0.6 reduce-window.19
  3.5 0.2 slice_reduce_fusion.1
  3.8 0.6 copy-done.15
  4.4 0.2 slice_reduce_fusion.3
  4.6 0.8 reduce-window.16
  5.5 0.5 slice.70
  6.0 0.1 convert_reduce_fusion
  6.1 0.6 slice.66
  7.3 0.6 fusion.72
  7.9 1.6 copy.59
  9.5 2.1 copy.58
  11.6 1.4 broadcast_compare_fusion.1
  13.1 0.1 multiply_bitcast_fusion
  13.2 0.2 slice_reduce_fusion.2
  13.4 0.4 convert_multiply_fusion.2
  13.8 1.6 convolution_bitcast_fusion
  15.5 0.4 convert_multiply_fusion.4
  15.9 1.5 copy-done.2
  17.4 1.6 convolution_bitcast_fusion.1
  19.0 1.7 pad_maximum_fusion
  20.8 12.0 %all-to-all-start = ((f32[32,8,2688]{2,1,0:T(8,128)}), f32[32,8,2688]{2,1,0:T(8,128)S(1)}, u32[]{:S(2)}, u32[]{:S(2)}) async-start(f32[32,8,2688]{2,1,0:T(8,128)} %pad_maximum_fusion), calls=%async_computation | async-start | bytes 5505024 | tf_op jit(solution)/shard_map/all_to_all | solution.py:47
  32.8 62.4 %all-to-all-done = f32[32,8,2688]{2,1,0:T(8,128)S(1)} async-done(((f32[32,8,2688]{2,1,0:T(8,128)}), f32[32,8,2688]{2,1,0:T(8,128)S(1)}, u32[]{:S(2)}, u32[]{:S(2)}) %all-to-all-start) | async-done | bytes 2752544 | tf_op jit(solution)/shard_map/all_to_all | solution.py:47
  95.3 1.1 broadcast_in_dim.64
  96.3 1.5 broadcast_in_dim_reshape.3
  97.8 3.4 %conditional.1 = (f32[32,8,2560]{2,1,0:T(8,128)}) conditional(s32[]{:T(128)} %convert_element_type.65, (f32[32,8,2688]{2,1,0:T(8,128)S(1)}, f32[32,1,2560]{2,1,0:T(1,128)S(1)}) %tuple.26, (f32[32,8,2688]{2,1,0:T(8,128)S(1)}, f32[32,1,2560]{2,1,0:T(1,128)S(1)}) %tuple.26), branch_computations={%region_5.6_spmd, %region_6.7_spmd} | conditional | bytes 8 | solution.py:63
  97.9 3.4 %branch_1_fun.1 = f32[32,8,2560]{2,1,0:T(8,128)} custom-call(f32[32,8,2688]{2,1,0:T(8,128)S(1)} %get-tuple-element.25.moved_ref, f32[32,1,2560]{2,1,0:T(1,128)S(1)} %get-tuple-element.26.decay_ref), custom_call_target="tpu_custom_call" | custom-call | tf_op jit(solution)/shard_map/cond/branch_1_fun/pallas_call | solution.py:63
  101.3 7.1 %all-to-all-start.1 = ((f32[32,8,2560]{2,1,0:T(8,128)}), f32[32,8,2560]{2,1,0:T(8,128)S(1)}, u32[]{:S(2)}, u32[]{:S(2)}) async-start(f32[32,8,2560]{2,1,0:T(8,128)} %get-tuple-element.71), calls=%async_computation.1 | async-start | bytes 5242880 | tf_op jit(solution)/shard_map/all_to_all | solution.py:70
  108.4 2.1 multiply_reduce_fusion.2
  110.5 0.7 reduce_sum.196
  111.2 0.1 fusion.44
  111.3 0.2 fusion.48
  111.5 55.6 %all-to-all-done.1 = f32[32,8,2560]{2,1,0:T(8,128)S(1)} async-done(((f32[32,8,2560]{2,1,0:T(8,128)}), f32[32,8,2560]{2,1,0:T(8,128)S(1)}, u32[]{:S(2)}, u32[]{:S(2)}) %all-to-all-start.1) | async-done | bytes 2621472 | tf_op jit(solution)/shard_map/all_to_all | solution.py:70
  167.2 1.2 fusion.26
  168.5 1.2 fusion.22
  169.7 1.0 copy-done.5
  170.7 0.4 copy-done.7
  171.1 1.9 fusion.13
  173.1 0.7 fusion.74
  173.8 9.4 %fusion.6 = (f32[40,256]{1,0:T(8,128)}, f32[40,256]{1,0:T(8,128)}, f32[40,256]{1,0:T(8,128)}, f32[256,256]{1,0:T(8,128)S(1)}) fusion(f32[40,256]{1,0:T(8,128)S(1)} %get-tuple-element.64, f32[256,256]{1,0:T(8,128)S(1)} %fusion.48, f32[40,256]{1,0:T(8,128)S(1)} %copy-done.16, pred[256,256]{1,0:T(8,128)(4,1)S(1)} %fusion.44, ...), kind=kOutput, calls=%fused_computation.9 | convolution fusion | flops 374769664 | bytes 3416064 | tf_op jit(solution)/shard_map/transpose(jvp(hts,shp->thp))/dot_general | solution.py:93
  183.3 0.3 fusion.51
  183.5 0.4 fusion.45
  184.0 0.8 copy.60
  184.8 0.1 multiply_reduce_fusion.3
  185.0 0.1 reduce_sum.160
  185.1 0.1 copy.61
  185.2 0.8 copy_bitcast_fusion.1
  186.0 2.5 %reduce-window.21 = f32[40,2,128]{2,0,1:T(8,128)S(1)} reduce-window(f32[40,2,128]{2,0,1:T(8,128)S(1)} %copy_bitcast_fusion.1, f32[]{:T(128)} %constant.67.clone.1), window={size=1x1x128 pad=0_0x0_0x0_127}, to_apply=%region_15.16 | reduce-window | flops 1300480 | bytes 81924 | tf_op jit(solution)/shard_map/reduce-window.3
  188.6 0.1 slice_reduce_fusion
  188.7 0.1 broadcast_add_fusion
  188.9 0.2 fusion.61
  189.1 0.7 multiply_bitcast_fusion.1
  189.7 1.5 fusion.75
  191.2 0.7 maximum_multiply_fusion
  191.9 0.1 mul.216
  192.0 0.7 broadcast_in_dim.110
  192.7 12.0 %all-to-all-start.2 = ((f32[256,1,128]{2,1,0:T(1,128)}), f32[256,1,128]{2,1,0:T(1,128)S(1)}, u32[]{:S(2)}, u32[]{:S(2)}) async-start(f32[256,1,128]{2,1,0:T(1,128)} %broadcast_in_dim.110), calls=%async_computation.2 | async-start | bytes 262144 | tf_op jit(solution)/shard_map/all_to_all | solution.py:218
  204.7 10.1 %fusion.16 = bf16[256,40,64]{0,2,1:T(8,128)(2,1)} fusion(bf16[256,40,64]{0,2,1:T(8,128)(2,1)} %bitcast.183, f32[256,40,64]{0,2,1:T(8,128)} %bitcast.191, bf16[40,64,256]{2,1,0:T(8,128)(2,1)} %bitcast.184, f32[40,256]{1,0:T(8,128)S(1)} %copy-done.23, f32[256,256]{1,0:T(8,128)} %copy-done.11, f32[40,256]{1,0:T(8,128)S(1)} %copy-done.17, ...), kind=kOutput, calls=%fused_computation.27 | convolution fusion | flops 2030305280 | bytes 7004320 | tf_op jit(solution)/shard_map/transpose(jvp(hts,shp->thp))/dot_general | solution.py:93
  214.9 2.4 %copy.66 = bf16[1,256,2560]{2,1,0:T(8,128)(2,1)} copy(bf16[1,256,2560]{1,2,0:T(8,128)(2,1)} %bitcast.193) | data formatting | bytes 2621440
  217.3 6.8 %fusion.41 = f32[1,256,128]{2,1,0:T(8,128)} fusion(f32[256,128]{1,0:T(8,128)S(1)} %fusion.51, f32[256,2560]{0,1:T(8,128)} %bitcast.179, f32[32,8,2560]{2,1,0:T(8,128)S(1)} %all-to-all-done.1), kind=kOutput, calls=%fused_computation.46 | convolution fusion | flops 1006665728 | bytes 4194304 | tf_op jit(solution)/shard_map/transpose(jvp())/dot_general | solution.py:97
  224.1 5.0 %fusion.35 = f32[1,256,128]{2,1,0:T(8,128)} fusion(f32[256,128]{1,0:T(8,128)S(1)} %fusion.45, f32[256,2560]{0,1:T(8,128)S(1)} %bitcast.181, f32[32,8,2560]{2,1,0:T(8,128)S(1)} %all-to-all-done.1), kind=kOutput, calls=%fused_computation.44 | convolution fusion | flops 1006665728 | bytes 4194304 | tf_op jit(solution)/shard_map/transpose(jvp())/dot_general | solution.py:111
  229.1 0.7 reshape.383
  (87 shorter events, 0.6 us)
Async XLA Ops:
  0.6 16.8 %copy-start = (bf16[1,256,128]{2,1,0:T(8,128)(2,1)S(1)}, bf16[1,256,128]{2,1,0:T(8,128)(2,1)}, u32[]{:S(2)}) copy-start(bf16[1,256,128]{2,1,0:T(8,128)(2,1)} %param.15) | copy-start | bytes 196612
  1.3 6.6 %copy-start.36 = (f32[40]{0:T(128)}, f32[40]{0:T(128)S(1)}, u32[]{:S(2)}) copy-start(f32[40]{0:T(128)S(1)} %exponential_negate_fusion) | copy-start | bytes 484
  3.7 9.4 %copy-start.25 = (f32[40,2]{0,1:T(2,128)}, f32[40,2]{0,1:T(2,128)S(1)}, u32[]{:S(2)}) copy-start(f32[40,2]{0,1:T(2,128)S(1)} %slice.68) | copy-start | bytes 964
  3.8 0.6 copy-start.15
  4.6 8.5 %copy-start.33 = (f32[40]{0:T(128)}, f32[40]{0:T(128)S(1)}, u32[]{:S(2)}) copy-start(f32[40]{0:T(128)S(1)} %slice_reduce_fusion.3) | copy-start | bytes 484
  7.9 5.2 %copy-start.9 = (f32[1,40,256]{2,1,0:T(8,128)S(1)}, f32[1,40,256]{2,1,0:T(8,128)}, u32[]{:S(2)}) copy-start(f32[1,40,256]{2,1,0:T(8,128)} %param.14) | copy-start | bytes 122884
  7.9 5.2 %copy-start.27 = (f32[40]{0:T(128)S(1)}, f32[40]{0:T(128)}, u32[]{:S(2)}) copy-start(f32[40]{0:T(128)} %param.18) | copy-start | bytes 484
  9.5 4.3 %copy-start.4 = (bf16[1,256,2560]{1,2,0:T(8,128)(2,1)}, bf16[1,256,2560]{1,2,0:T(8,128)(2,1)S(1)}, u32[]{:S(2)}) copy-start(bf16[1,256,2560]{1,2,0:T(8,128)(2,1)S(1)} %copy.59) | copy-start | bytes 3932164
  11.6 3.9 %copy-start.6 = (bf16[1,256,2560]{1,2,0:T(8,128)(2,1)}, bf16[1,256,2560]{1,2,0:T(8,128)(2,1)S(1)}, u32[]{:S(2)}) copy-start(bf16[1,256,2560]{1,2,0:T(8,128)(2,1)S(1)} %copy.58) | copy-start | bytes 3932164
  11.6 2.2 copy-start.10
  13.1 2.4 %copy-start.30 = (pred[256]{0:T(512)(128)(4,1)}, pred[256]{0:T(512)(128)(4,1)S(1)}, u32[]{:S(2)}) copy-start(pred[256]{0:T(512)(128)(4,1)S(1)} %get-tuple-element.67) | copy-start | bytes 772
  13.1 2.4 %copy-start.35 = (pred[256]{0:T(512)(128)(4,1)}, pred[256]{0:T(512)(128)(4,1)S(1)}, u32[]{:S(2)}) copy-start(pred[256]{0:T(512)(128)(4,1)S(1)} %get-tuple-element.68) | copy-start | bytes 772
  13.2 2.3 copy-start.12
  13.8 2.1 copy-start.1
  15.9 1.5 copy-start.2
  20.8 74.5 %all-to-all-start = ((f32[32,8,2688]{2,1,0:T(8,128)}), f32[32,8,2688]{2,1,0:T(8,128)S(1)}, u32[]{:S(2)}, u32[]{:S(2)}) async-start(f32[32,8,2688]{2,1,0:T(8,128)} %pad_maximum_fusion), calls=%async_computation | async-start | bytes 5505024 | tf_op jit(solution)/shard_map/all_to_all | solution.py:47
  101.3 65.9 %all-to-all-start.1 = ((f32[32,8,2560]{2,1,0:T(8,128)}), f32[32,8,2560]{2,1,0:T(8,128)S(1)}, u32[]{:S(2)}, u32[]{:S(2)}) async-start(f32[32,8,2560]{2,1,0:T(8,128)} %get-tuple-element.71), calls=%async_computation.1 | async-start | bytes 5242880 | tf_op jit(solution)/shard_map/all_to_all | solution.py:70
  111.3 62.5 %copy-start.18 = (pred[256,256]{1,0:T(8,128)(4,1)}, pred[256,256]{1,0:T(8,128)(4,1)S(1)}, u32[]{:S(2)}) copy-start(pred[256,256]{1,0:T(8,128)(4,1)S(1)} %fusion.44) | copy-start | bytes 196612
  111.5 62.3 %copy-start.11 = (f32[256,256]{1,0:T(8,128)}, f32[256,256]{1,0:T(8,128)S(1)}, u32[]{:S(2)}) copy-start(f32[256,256]{1,0:T(8,128)S(1)} %fusion.48) | copy-start | bytes 786436
  168.4 4.6 %copy-start.8 = (f32[2560,256]{1,0:T(8,128)}, f32[2560,256]{1,0:T(8,128)S(1)}, u32[]{:S(2)}) copy-start(f32[2560,256]{1,0:T(8,128)S(1)} %fusion.26) | copy-start | bytes 7864324
  168.4 2.3 copy-start.5
  168.5 2.6 %copy-start.7 = (bf16[1,256,2560]{1,2,0:T(8,128)(2,1)S(1)}, bf16[1,256,2560]{1,2,0:T(8,128)(2,1)}, u32[]{:S(2)}) copy-start(bf16[1,256,2560]{1,2,0:T(8,128)(2,1)} %copy-done.6) | copy-start | bytes 3932164
  171.1 1.9 copy-start.26
  171.1 1.9 copy-start.28
  171.1 1.9 copy-start.31
  171.1 1.9 copy-start.34
  171.1 2.7 %copy-start.16 = (f32[40,256]{1,0:T(8,128)S(1)}, f32[40,256]{1,0:T(8,128)}, u32[]{:S(2)}) copy-start(f32[40,256]{1,0:T(8,128)} %copy-done.15) | copy-start | bytes 122884
  173.8 9.5 %copy-start.22 = (f32[40,256]{1,0:T(8,128)}, f32[40,256]{1,0:T(8,128)S(1)}, u32[]{:S(2)}) copy-start(f32[40,256]{1,0:T(8,128)S(1)} %get-tuple-element.64) | copy-start | bytes 122884
  183.2 2.0 copy-start.14
  183.2 2.0 copy-start.29
  183.2 2.0 copy-start.32
  183.3 21.5 %copy-start.13 = (f32[256,40]{0,1:T(8,128)S(1)}, f32[256,40]{0,1:T(8,128)}, u32[]{:S(2)}) copy-start(f32[256,40]{0,1:T(8,128)} %copy-done.12) | copy-start | bytes 122884
  183.3 21.5 %copy-start.17 = (f32[40,256]{1,0:T(8,128)S(1)}, f32[40,256]{1,0:T(8,128)}, u32[]{:S(2)}) copy-start(f32[40,256]{1,0:T(8,128)} %copy-done.15) | copy-start | bytes 122884
  183.9 1.3 copy-start.20
  183.9 1.3 copy-start.21
  184.0 5.8 %copy-start.24 = (f32[40,256]{1,0:T(8,128)S(1)}, f32[40,256]{1,0:T(8,128)}, u32[]{:S(2)}) copy-start(f32[40,256]{1,0:T(8,128)} %get-tuple-element.59) | copy-start | bytes 122884
  184.0 20.8 %copy-start.19 = (pred[256,256]{1,0:T(8,128)(4,1)S(1)}, pred[256,256]{1,0:T(8,128)(4,1)}, u32[]{:S(2)}) copy-start(pred[256,256]{1,0:T(8,128)(4,1)} %copy-done.18) | copy-start | bytes 196612
  184.0 20.8 %copy-start.23 = (f32[40,256]{1,0:T(8,128)S(1)}, f32[40,256]{1,0:T(8,128)}, u32[]{:S(2)}) copy-start(f32[40,256]{1,0:T(8,128)} %copy-done.22) | copy-start | bytes 122884
  192.7 36.4 %all-to-all-start.2 = ((f32[256,1,128]{2,1,0:T(1,128)}), f32[256,1,128]{2,1,0:T(1,128)S(1)}, u32[]{:S(2)}, u32[]{:S(2)}) async-start(f32[256,1,128]{2,1,0:T(1,128)} %broadcast_in_dim.110), calls=%async_computation.2 | async-start | bytes 262144 | tf_op jit(solution)/shard_map/all_to_all | solution.py:218
  217.3 6.8 %copy-start.3 = (f32[256,40,64]{0,2,1:T(8,128)S(1)}, f32[256,40,64]{0,2,1:T(8,128)}, u32[]{:S(2)}) copy-start(f32[256,40,64]{0,2,1:T(8,128)} %copy-done.2) | copy-start | bytes 7864324
where the time goes:
time: 231 us; the launch traced here: 230 us
  waiting for transfers between devices  118 us (51%)
  matrix products  37.9 us (16%)
  starting transfers between devices  31.1 us (13%)
  other arithmetic  20 us (9%)
  local copies, waits for them, and re-layouts  17.4 us (8%)
  Pallas kernels  3.42 us (1%)
    all_to_all x1, waiting for transfers between devices, exchange_scan(): lax.all_to_all(jnp.concatenate([sent, extra], axis=2), axis, 0, 0, tiled=...  62.4 us
    all_to_all x1, waiting for transfers between devices, exchange_scan(): back = lax.all_to_all(scanned, axis, 0, 0, tiled=True)  55.6 us
    dot_general x2, matrix products, group_step(): inner = jnp.einsum('hts,shp->thp', weights, inputs, precision=HIGH)  19.6 us
    all_to_all x1, starting transfers between devices, exchange_scan(): lax.all_to_all(jnp.concatenate([sent, extra], axis=2), axis, 0, 0, tiled=...  12 us
    all_to_all x1, starting transfers between devices, shards(): lax.all_to_all(spread, ('dp', 'ctx'), 0, 0, tiled=True)  12 us
    unnamed x77, local copies, waits for them, and re-layouts  9.75 us
    dot_general x2, matrix products, group_step(): jnp.dot(reader_piece, state.reshape(rows, heads * head_size), precision=H...  8.04 us
    all_to_all x1, starting transfers between devices, exchange_scan(): back = lax.all_to_all(scanned, axis, 0, 0, tiled=True)  7.09 us
  transfers between devices with their start and end apart: 3, of which 2 were waited for; matrix products, arithmetic and copies ran while one was open for 12% of the time, Pallas kernels for 0%

commit v1 on v0

--- a/solution.py
+++ b/solution.py
@@ -7,7 +7,7 @@
 SPAN = 256
 
 
-HIGH = lax.Precision.HIGHEST
+HIGH = lax.Precision.HIGH
 
 
 def forward_kernel(moved_ref, decay_ref, out_ref):

time: 231 us -> 223 us (0.965)
  matrix products: 37.9 us -> 29.8 us
    dot_general x2, matrix products: 6.23 us -> 3.81 us  [group_step(): jnp.dot(writer_piece.T, (to_end.T[:, :, None] * inputs).reshape(size, hea...]
    dot_general x2, matrix products: 8.04 us -> 5.66 us  [group_step(): jnp.dot(reader_piece, state.reshape(rows, heads * head_size), precision=H...]
  transfers between devices with their start and end apart: 3 -> 3, of which waited for: 2 -> 2; matrix products, arithmetic and copies ran while one was open for 12% -> 10% of each run, Pallas kernels for 0% -> 0%
where the time goes in v1:
time: 223 us; the launch traced here: 222 us
  waiting for transfers between devices  118 us (53%)
  starting transfers between devices  31.1 us (14%)
  matrix products  29.8 us (13%)
  other arithmetic  20 us (9%)
  local copies, waits for them, and re-layouts  17.8 us (8%)
  Pallas kernels  3.42 us (2%)
    all_to_all x1, waiting for transfers between devices, exchange_scan(): lax.all_to_all(jnp.concatenate([sent, extra], axis=2), axis, 0, 0, tiled=...  62.4 us
    all_to_all x1, waiting for transfers between devices, exchange_scan(): back = lax.all_to_all(scanned, axis, 0, 0, tiled=True)  55.6 us
    dot_general x2, matrix products, group_step(): inner = jnp.einsum('hts,shp->thp', weights, inputs, precision=HIGH)  17.5 us
    all_to_all x1, starting transfers between devices, exchange_scan(): lax.all_to_all(jnp.concatenate([sent, extra], axis=2), axis, 0, 0, tiled=...  12 us
    all_to_all x1, starting transfers between devices, shards(): lax.all_to_all(spread, ('dp', 'ctx'), 0, 0, tiled=True)  12 us
    unnamed x77, local copies, waits for them, and re-layouts  10.1 us
    all_to_all x1, starting transfers between devices, exchange_scan(): back = lax.all_to_all(scanned, axis, 0, 0, tiled=True)  7.09 us
    dot_general x2, matrix products, group_step(): jnp.dot(reader_piece, state.reshape(rows, heads * head_size), precision=H...  5.66 us
  transfers between devices with their start and end apart: 3, of which 2 were waited for; matrix products, arithmetic and copies ran while one was open for 10% of the time, Pallas kernels for 0%

profile of v1, /device:TPU:1, one launch (start us, length us, event | category | flops | bytes accessed | tf_op | source)
XLA Modules:
  0.0 222.1 jit_solution(4856107588257617407)
XLA Ops:
  0.6 0.7 exponential_negate_fusion
  1.3 0.8 squeeze.28
  2.2 0.8 fusion.56
  2.9 0.6 reduce-window.19
  3.5 0.2 slice_reduce_fusion.1
  3.8 0.6 copy-done.15
  4.4 0.2 slice_reduce_fusion.3
  4.6 0.8 reduce-window.16
  5.5 0.5 slice.70
  6.0 0.1 convert_reduce_fusion
  6.1 0.6 slice.66
  7.3 0.6 fusion.72
  7.9 1.6 copy.59
  9.5 2.1 copy.58
  11.6 1.4 broadcast_compare_fusion.1
  13.1 0.1 multiply_bitcast_fusion
  13.2 0.2 slice_reduce_fusion.2
  13.4 0.4 convert_multiply_fusion.2
  13.8 1.0 convolution_bitcast_fusion
  14.9 0.4 convert_multiply_fusion.4
  15.3 1.5 copy-done.2
  16.8 1.0 convolution_bitcast_fusion.1
  17.9 1.7 pad_maximum_fusion
  19.6 12.0 %all-to-all-start = ((f32[32,8,2688]{2,1,0:T(8,128)}), f32[32,8,2688]{2,1,0:T(8,128)S(1)}, u32[]{:S(2)}, u32[]{:S(2)}) async-start(f32[32,8,2688]{2,1,0:T(8,128)} %pad_maximum_fusion), calls=%async_computation | async-start | bytes 5505024 | tf_op jit(solution)/shard_map/all_to_all | solution.py:47
  31.7 62.4 %all-to-all-done = f32[32,8,2688]{2,1,0:T(8,128)S(1)} async-done(((f32[32,8,2688]{2,1,0:T(8,128)}), f32[32,8,2688]{2,1,0:T(8,128)S(1)}, u32[]{:S(2)}, u32[]{:S(2)}) %all-to-all-start) | async-done | bytes 2752544 | tf_op jit(solution)/shard_map/all_to_all | solution.py:47
  94.1 1.1 broadcast_in_dim.64
  95.2 1.5 broadcast_in_dim_reshape.3
  96.7 3.4 %conditional.1 = (f32[32,8,2560]{2,1,0:T(8,128)}) conditional(s32[]{:T(128)} %convert_element_type.65, (f32[32,8,2688]{2,1,0:T(8,128)S(1)}, f32[32,1,2560]{2,1,0:T(1,128)S(1)}) %tuple.26, (f32[32,8,2688]{2,1,0:T(8,128)S(1)}, f32[32,1,2560]{2,1,0:T(1,128)S(1)}) %tuple.26), branch_computations={%region_5.6_spmd, %region_6.7_spmd} | conditional | bytes 8 | solution.py:63
  96.7 3.4 %branch_1_fun.1 = f32[32,8,2560]{2,1,0:T(8,128)} custom-call(f32[32,8,2688]{2,1,0:T(8,128)S(1)} %get-tuple-element.25.moved_ref, f32[32,1,2560]{2,1,0:T(1,128)S(1)} %get-tuple-element.26.decay_ref), custom_call_target="tpu_custom_call" | custom-call | tf_op jit(solution)/shard_map/cond/branch_1_fun/pallas_call | solution.py:63
  100.1 7.1 %all-to-all-start.1 = ((f32[32,8,2560]{2,1,0:T(8,128)}), f32[32,8,2560]{2,1,0:T(8,128)S(1)}, u32[]{:S(2)}, u32[]{:S(2)}) async-start(f32[32,8,2560]{2,1,0:T(8,128)} %get-tuple-element.71), calls=%async_computation.1 | async-start | bytes 5242880 | tf_op jit(solution)/shard_map/all_to_all | solution.py:70
  107.2 2.1 multiply_reduce_fusion.2
  109.4 0.7 reduce_sum.196
  110.1 0.1 fusion.44
  110.2 0.2 fusion.48
  110.4 55.6 %all-to-all-done.1 = f32[32,8,2560]{2,1,0:T(8,128)S(1)} async-done(((f32[32,8,2560]{2,1,0:T(8,128)}), f32[32,8,2560]{2,1,0:T(8,128)S(1)}, u32[]{:S(2)}, u32[]{:S(2)}) %all-to-all-start.1) | async-done | bytes 2621472 | tf_op jit(solution)/shard_map/all_to_all | solution.py:70
  166.0 0.9 fusion.26
  167.0 0.9 fusion.22
  167.9 1.4 copy-done.5
  169.2 0.4 copy-done.7
  169.6 1.9 fusion.13
  171.6 0.7 fusion.74
  172.3 9.4 %fusion.6 = (f32[40,256]{1,0:T(8,128)}, f32[40,256]{1,0:T(8,128)}, f32[40,256]{1,0:T(8,128)}, f32[256,256]{1,0:T(8,128)S(1)}) fusion(f32[40,256]{1,0:T(8,128)S(1)} %get-tuple-element.64, f32[256,256]{1,0:T(8,128)S(1)} %fusion.48, f32[40,256]{1,0:T(8,128)S(1)} %copy-done.16, pred[256,256]{1,0:T(8,128)(4,1)S(1)} %fusion.44, ...), kind=kOutput, calls=%fused_computation.9 | convolution fusion | flops 374769664 | bytes 3416064 | tf_op jit(solution)/shard_map/transpose(jvp(hts,shp->thp))/dot_general | solution.py:93
  181.8 0.2 fusion.51
  182.0 0.3 fusion.45
  182.4 0.8 copy.60
  183.2 0.1 multiply_reduce_fusion.3
  183.4 0.1 reduce_sum.160
  183.5 0.1 copy.61
  183.6 0.8 copy_bitcast_fusion.1
  184.4 2.5 %reduce-window.21 = f32[40,2,128]{2,0,1:T(8,128)S(1)} reduce-window(f32[40,2,128]{2,0,1:T(8,128)S(1)} %copy_bitcast_fusion.1, f32[]{:T(128)} %constant.67.clone.1), window={size=1x1x128 pad=0_0x0_0x0_127}, to_apply=%region_15.16 | reduce-window | flops 1300480 | bytes 81924 | tf_op jit(solution)/shard_map/reduce-window.3
  187.0 0.1 slice_reduce_fusion
  187.1 0.1 broadcast_add_fusion
  187.3 0.2 fusion.61
  187.5 0.7 multiply_bitcast_fusion.1
  188.1 1.5 fusion.75
  189.6 0.7 maximum_multiply_fusion
  190.3 0.1 mul.216
  190.4 0.7 broadcast_in_dim.110
  191.1 12.0 %all-to-all-start.2 = ((f32[256,1,128]{2,1,0:T(1,128)}), f32[256,1,128]{2,1,0:T(1,128)S(1)}, u32[]{:S(2)}, u32[]{:S(2)}) async-start(f32[256,1,128]{2,1,0:T(1,128)} %broadcast_in_dim.110), calls=%async_computation.2 | async-start | bytes 262144 | tf_op jit(solution)/shard_map/all_to_all | solution.py:218
  203.1 8.1 %fusion.16 = bf16[256,40,64]{0,2,1:T(8,128)(2,1)} fusion(bf16[256,40,64]{0,2,1:T(8,128)(2,1)} %bitcast.183, f32[256,40,64]{0,2,1:T(8,128)} %bitcast.191, bf16[40,64,256]{2,1,0:T(8,128)(2,1)} %bitcast.184, f32[40,256]{1,0:T(8,128)S(1)} %copy-done.23, f32[256,256]{1,0:T(8,128)} %copy-done.11, f32[40,256]{1,0:T(8,128)S(1)} %copy-done.17, ...), kind=kOutput, calls=%fused_computation.27 | convolution fusion | flops 1023672320 | bytes 7004320 | tf_op jit(solution)/shard_map/transpose(jvp(hts,shp->thp))/dot_general | solution.py:93
  211.2 2.4 %copy.66 = bf16[1,256,2560]{2,1,0:T(8,128)(2,1)} copy(bf16[1,256,2560]{1,2,0:T(8,128)(2,1)} %bitcast.193) | data formatting | bytes 2621440
  213.7 4.8 %fusion.41 = f32[1,256,128]{2,1,0:T(8,128)} fusion(f32[256,128]{1,0:T(8,128)S(1)} %fusion.51, f32[256,2560]{0,1:T(8,128)} %bitcast.179, f32[32,8,2560]{2,1,0:T(8,128)S(1)} %all-to-all-done.1), kind=kOutput, calls=%fused_computation.46 | convolution fusion | flops 503349248 | bytes 4194304 | tf_op jit(solution)/shard_map/transpose(jvp())/dot_general | solution.py:97
  218.4 2.9 %fusion.35 = f32[1,256,128]{2,1,0:T(8,128)} fusion(f32[256,128]{1,0:T(8,128)S(1)} %fusion.45, f32[256,2560]{0,1:T(8,128)S(1)} %bitcast.181, f32[32,8,2560]{2,1,0:T(8,128)S(1)} %all-to-all-done.1), kind=kOutput, calls=%fused_computation.44 | convolution fusion | flops 503349248 | bytes 4194304 | tf_op jit(solution)/shard_map/transpose(jvp())/dot_general | solution.py:111
  221.4 0.7 reshape.383
  (87 shorter events, 0.6 us)
Async XLA Ops:
  0.6 16.2 %copy-start = (bf16[1,256,128]{2,1,0:T(8,128)(2,1)S(1)}, bf16[1,256,128]{2,1,0:T(8,128)(2,1)}, u32[]{:S(2)}) copy-start(bf16[1,256,128]{2,1,0:T(8,128)(2,1)} %param.15) | copy-start | bytes 196612
  1.3 6.6 %copy-start.36 = (f32[40]{0:T(128)}, f32[40]{0:T(128)S(1)}, u32[]{:S(2)}) copy-start(f32[40]{0:T(128)S(1)} %exponential_negate_fusion) | copy-start | bytes 484
  3.7 9.4 %copy-start.25 = (f32[40,2]{0,1:T(2,128)}, f32[40,2]{0,1:T(2,128)S(1)}, u32[]{:S(2)}) copy-start(f32[40,2]{0,1:T(2,128)S(1)} %slice.68) | copy-start | bytes 964
  3.8 0.6 copy-start.15
  4.6 8.5 %copy-start.33 = (f32[40]{0:T(128)}, f32[40]{0:T(128)S(1)}, u32[]{:S(2)}) copy-start(f32[40]{0:T(128)S(1)} %slice_reduce_fusion.3) | copy-start | bytes 484
  7.9 5.2 %copy-start.9 = (f32[1,40,256]{2,1,0:T(8,128)S(1)}, f32[1,40,256]{2,1,0:T(8,128)}, u32[]{:S(2)}) copy-start(f32[1,40,256]{2,1,0:T(8,128)} %param.14) | copy-start | bytes 122884
  7.9 5.2 %copy-start.27 = (f32[40]{0:T(128)S(1)}, f32[40]{0:T(128)}, u32[]{:S(2)}) copy-start(f32[40]{0:T(128)} %param.18) | copy-start | bytes 484
  9.5 4.3 %copy-start.4 = (bf16[1,256,2560]{1,2,0:T(8,128)(2,1)}, bf16[1,256,2560]{1,2,0:T(8,128)(2,1)S(1)}, u32[]{:S(2)}) copy-start(bf16[1,256,2560]{1,2,0:T(8,128)(2,1)S(1)} %copy.59) | copy-start | bytes 3932164
  11.6 3.3 %copy-start.6 = (bf16[1,256,2560]{1,2,0:T(8,128)(2,1)}, bf16[1,256,2560]{1,2,0:T(8,128)(2,1)S(1)}, u32[]{:S(2)}) copy-start(bf16[1,256,2560]{1,2,0:T(8,128)(2,1)S(1)} %copy.58) | copy-start | bytes 3932164
  11.6 2.2 copy-start.10
  13.1 1.8 copy-start.30
  13.1 1.8 copy-start.35
  13.2 1.7 copy-start.12
  13.8 1.5 copy-start.1
  15.3 1.5 copy-start.2
  19.6 74.5 %all-to-all-start = ((f32[32,8,2688]{2,1,0:T(8,128)}), f32[32,8,2688]{2,1,0:T(8,128)S(1)}, u32[]{:S(2)}, u32[]{:S(2)}) async-start(f32[32,8,2688]{2,1,0:T(8,128)} %pad_maximum_fusion), calls=%async_computation | async-start | bytes 5505024 | tf_op jit(solution)/shard_map/all_to_all | solution.py:47
  100.1 65.9 %all-to-all-start.1 = ((f32[32,8,2560]{2,1,0:T(8,128)}), f32[32,8,2560]{2,1,0:T(8,128)S(1)}, u32[]{:S(2)}, u32[]{:S(2)}) async-start(f32[32,8,2560]{2,1,0:T(8,128)} %get-tuple-element.71), calls=%async_computation.1 | async-start | bytes 5242880 | tf_op jit(solution)/shard_map/all_to_all | solution.py:70
  110.2 62.1 %copy-start.18 = (pred[256,256]{1,0:T(8,128)(4,1)}, pred[256,256]{1,0:T(8,128)(4,1)S(1)}, u32[]{:S(2)}) copy-start(pred[256,256]{1,0:T(8,128)(4,1)S(1)} %fusion.44) | copy-start | bytes 196612
  110.4 61.9 %copy-start.11 = (f32[256,256]{1,0:T(8,128)}, f32[256,256]{1,0:T(8,128)S(1)}, u32[]{:S(2)}) copy-start(f32[256,256]{1,0:T(8,128)S(1)} %fusion.48) | copy-start | bytes 786436
  166.9 4.6 %copy-start.8 = (f32[2560,256]{1,0:T(8,128)}, f32[2560,256]{1,0:T(8,128)S(1)}, u32[]{:S(2)}) copy-start(f32[2560,256]{1,0:T(8,128)S(1)} %fusion.26) | copy-start | bytes 7864324
  166.9 2.3 %copy-start.5 = (bf16[1,256,2560]{1,2,0:T(8,128)(2,1)S(1)}, bf16[1,256,2560]{1,2,0:T(8,128)(2,1)}, u32[]{:S(2)}) copy-start(bf16[1,256,2560]{1,2,0:T(8,128)(2,1)} %copy-done.4) | copy-start | bytes 3932164
  167.0 2.6 %copy-start.7 = (bf16[1,256,2560]{1,2,0:T(8,128)(2,1)S(1)}, bf16[1,256,2560]{1,2,0:T(8,128)(2,1)}, u32[]{:S(2)}) copy-start(bf16[1,256,2560]{1,2,0:T(8,128)(2,1)} %copy-done.6) | copy-start | bytes 3932164
  169.6 1.9 copy-start.26
  169.6 1.9 copy-start.28
  169.6 1.9 copy-start.31
  169.6 1.9 copy-start.34
  169.6 2.7 %copy-start.16 = (f32[40,256]{1,0:T(8,128)S(1)}, f32[40,256]{1,0:T(8,128)}, u32[]{:S(2)}) copy-start(f32[40,256]{1,0:T(8,128)} %copy-done.15) | copy-start | bytes 122884
  172.3 9.5 %copy-start.22 = (f32[40,256]{1,0:T(8,128)}, f32[40,256]{1,0:T(8,128)S(1)}, u32[]{:S(2)}) copy-start(f32[40,256]{1,0:T(8,128)S(1)} %get-tuple-element.64) | copy-start | bytes 122884
  181.7 1.9 copy-start.14
  181.7 1.9 copy-start.29
  181.8 1.9 copy-start.32
  181.8 21.4 %copy-start.13 = (f32[256,40]{0,1:T(8,128)S(1)}, f32[256,40]{0,1:T(8,128)}, u32[]{:S(2)}) copy-start(f32[256,40]{0,1:T(8,128)} %copy-done.12) | copy-start | bytes 122884
  181.8 21.4 %copy-start.17 = (f32[40,256]{1,0:T(8,128)S(1)}, f32[40,256]{1,0:T(8,128)}, u32[]{:S(2)}) copy-start(f32[40,256]{1,0:T(8,128)} %copy-done.15) | copy-start | bytes 122884
  182.3 1.3 copy-start.20
  182.3 1.3 copy-start.21
  182.4 5.8 %copy-start.24 = (f32[40,256]{1,0:T(8,128)S(1)}, f32[40,256]{1,0:T(8,128)}, u32[]{:S(2)}) copy-start(f32[40,256]{1,0:T(8,128)} %get-tuple-element.59) | copy-start | bytes 122884
  182.4 20.8 %copy-start.19 = (pred[256,256]{1,0:T(8,128)(4,1)S(1)}, pred[256,256]{1,0:T(8,128)(4,1)}, u32[]{:S(2)}) copy-start(pred[256,256]{1,0:T(8,128)(4,1)} %copy-done.18) | copy-start | bytes 196612
  182.4 20.8 %copy-start.23 = (f32[40,256]{1,0:T(8,128)S(1)}, f32[40,256]{1,0:T(8,128)}, u32[]{:S(2)}) copy-start(f32[40,256]{1,0:T(8,128)} %copy-done.22) | copy-start | bytes 122884
  191.1 30.2 %all-to-all-start.2 = ((f32[256,1,128]{2,1,0:T(1,128)}), f32[256,1,128]{2,1,0:T(1,128)S(1)}, u32[]{:S(2)}, u32[]{:S(2)}) async-start(f32[256,1,128]{2,1,0:T(1,128)} %broadcast_in_dim.110), calls=%async_computation.2 | async-start | bytes 262144 | tf_op jit(solution)/shard_map/all_to_all | solution.py:218
  213.7 4.8 %copy-start.3 = (f32[256,40,64]{0,2,1:T(8,128)S(1)}, f32[256,40,64]{0,2,1:T(8,128)}, u32[]{:S(2)}) copy-start(f32[256,40,64]{0,2,1:T(8,128)} %copy-done.2) | copy-start | bytes 7864324
